TPU v7x, 512 devices: a whole 4x8x8 slice. The times are simulated.
512 devices in a mesh: seq: 64 (over y, x, core), ch: 8 (over z).
Axes of the slice: x: 4, y: 8, z: 8, core: 2. Of those that a mesh axis runs over, the one named last changes fastest.
Arguments:
- signal: bfloat16 [1536, 32768], P('ch', 'seq'), may hold values from -16 to 16
- input_norm_gain: float32 [1536], P('ch'), may hold values from 0.25 to 1.75
- value_weight: bfloat16 [1536, 1536], P('seq', 'ch'), may hold values from -0.15625 to 0.15625
- gate_weight: bfloat16 [1536, 1536], P('seq', 'ch'), may hold values from -0.15625 to 0.15625
- depth_taps: float32 [31, 1536], P(None, 'ch'), may hold values from -1 to 1
- cotangent: bfloat16 [1536, 32768], P('ch', 'seq'), may hold values from -6 to 6
Outputs:
- output: bfloat16 [1536, 32768], P('ch', 'seq')
- signal_gradient: bfloat16 [1536, 32768], P('ch', 'seq')
- grad_value: float32 [1536, 1536], P('seq', 'ch')
- grad_gate: float32 [1536, 1536], P('seq', 'ch')
- grad_taps: float32 [31, 1536], P(None, 'ch')
- gain_gradient: float32 [1536], P('ch')
All inputs are finite; a program needn't handle non-finite values.
Results may differ from a plain program's by a relative error of at most 0.02.
Values may be sent and summed in bfloat16 or wider, within the bound.
No kernel may reach another device: no remote copies, remote signals or barrier semaphores. Data moves between devices by JAX's collectives and lax.ppermute only.
A program may use at most 64 MiB of HBM per device.

v0:
```python
import jax
import jax.numpy as jnp
from jax import lax
from jax.sharding import PartitionSpec as P


def extended(cells, sides, width):
    for axis, dim in sides:
        count = lax.axis_size(axis)
        ends = count - 1
        head = lax.slice_in_dim(cells, 0, width, axis=dim)
        tail = lax.slice_in_dim(cells, cells.shape[dim] - width, cells.shape[dim], axis=dim)
        cells = jnp.concatenate(
            [
                lax.ppermute(tail, axis, [(i, (i + 1) % count) for i in range(ends)]),
                cells,
                lax.ppermute(head, axis, [((i + 1) % count, i) for i in range(ends)]),
            ],
            axis=dim,
        )
    return cells


def standardize_rows(columns_in):
    values = columns_in.astype(jnp.float32)
    average = jnp.mean(values, 0, keepdims=True)
    centred = values - average
    spread = jnp.mean(centred * centred, 0, keepdims=True)
    inverse_deviation = lax.rsqrt(spread + 1e-05)
    return (centred * inverse_deviation, inverse_deviation)


def depthwise(padded, kernel):
    channels = padded.shape[0]
    result = lax.conv_general_dilated(
        padded[None],
        kernel,
        (1,),
        "VALID",
        dimension_numbers=("NCH", "OIH", "NCH"),
        feature_group_count=channels,
        precision=lax.Precision.HIGHEST,
    )
    return result[0]


def shards(signal, input_norm_gain, value_weight, gate_weight, depth_taps, cotangent):
    local_cols = signal.shape[0]
    seq_position = lax.axis_index("seq")
    channel_position = lax.axis_index("ch")
    reach = depth_taps.shape[0] // 2
    complete_signal = lax.all_gather(signal, "ch", axis=0, tiled=True)
    complete_gain = lax.all_gather(input_norm_gain, "ch", axis=0, tiled=True)
    centered_unit, inverse_deviation = standardize_rows(complete_signal)
    normalized_signal = (centered_unit * complete_gain[:, None]).astype(jnp.bfloat16)
    centered_unit_rows = lax.dynamic_slice_in_dim(
        centered_unit, channel_position * local_cols, local_cols, 0
    )
    stacked = jnp.concatenate([value_weight, gate_weight], 1)
    gathered = lax.all_gather(stacked, "seq", axis=0, tiled=True)
    mixed = lax.dot_general(
        gathered, normalized_signal, (((0,), (0,)), ((), ())), preferred_element_type=jnp.float32
    )
    value = mixed[:local_cols]
    gate = mixed[local_cols:]
    sig_gate = jax.nn.sigmoid(gate)
    glued = (value * sig_gate).astype(jnp.bfloat16)
    glued_pad = extended(glued, (("seq", 1),), reach).astype(jnp.float32)
    forward_kernel = depth_taps.T[:, None, :]
    pre = depthwise(glued_pad, forward_kernel)
    sig_pre = jax.nn.sigmoid(pre)
    output = (pre * sig_pre).astype(jnp.bfloat16)
    grad_pre = (cotangent.astype(jnp.float32) * sig_pre * (1.0 + pre * (1.0 - sig_pre))).astype(
        jnp.bfloat16
    )
    grad_pre_f = grad_pre.astype(jnp.float32)
    grad_pad = extended(grad_pre, (("seq", 1),), reach).astype(jnp.float32)
    grad_glued = depthwise(grad_pad, forward_kernel[:, :, ::-1])
    tap_partial = depthwise(glued_pad, grad_pre_f[:, None, :]).T
    grad_v = (grad_glued * sig_gate).astype(jnp.bfloat16)
    grad_g = (grad_glued * value * sig_gate * (1.0 - sig_gate)).astype(jnp.bfloat16)
    grad_both = jnp.concatenate([grad_v, grad_g], 0)
    weight_partial = lax.dot_general(
        normalized_signal, grad_both, (((1,), (1,)), ((), ())), preferred_element_type=jnp.float32
    )
    normed_term = jnp.dot(gathered, grad_both, preferred_element_type=jnp.float32)
    normalized_gradient = lax.psum_scatter(
        normed_term.astype(jnp.bfloat16), "ch", scatter_dimension=0, tiled=True
    ).astype(jnp.float32)
    scaled_signal = normalized_gradient * input_norm_gain[:, None]
    moments = jnp.concatenate(
        [
            jnp.sum(scaled_signal, 0, keepdims=True),
            jnp.sum(scaled_signal * centered_unit_rows, 0, keepdims=True),
        ],
        0,
    )
    moments = lax.psum(moments, "ch") * (1.0 / complete_signal.shape[0])
    inverse_rows = inverse_deviation
    signal_gradient = (
        inverse_rows * (scaled_signal - moments[0:1] - centered_unit_rows * moments[1:2])
    ).astype(jnp.bfloat16)
    gain_portion = jnp.sum(normalized_gradient * centered_unit_rows, 1)
    extra = jnp.concatenate([tap_partial, gain_portion[None]], 0)
    extra = jnp.pad(extra, ((0, 0), (0, weight_partial.shape[1] - extra.shape[1])))
    summed = lax.psum(jnp.concatenate([weight_partial, extra], 0), "seq")
    rows = value_weight.shape[0]
    weight_sums = lax.dynamic_slice_in_dim(summed, seq_position * rows, rows, 0)
    grad_value = weight_sums[:, :local_cols]
    grad_gate = weight_sums[:, local_cols:]
    taps_rows = depth_taps.shape[0]
    full_rows = weight_partial.shape[0]
    grad_taps = summed[full_rows : full_rows + taps_rows, :local_cols]
    gain_gradient = summed[full_rows + taps_rows, :local_cols]
    return (output, signal_gradient, grad_value, grad_gate, grad_taps, gain_gradient)


def solution(mesh):
    placed = (
        P("ch", "seq"),
        P("ch"),
        P("seq", "ch"),
        P("seq", "ch"),
        P(None, "ch"),
        P("ch", "seq"),
    )
    return jax.shard_map(
        shards,
        mesh=mesh,
        in_specs=placed,
        out_specs=(
            P("ch", "seq"),
            P("ch", "seq"),
            P("seq", "ch"),
            P("seq", "ch"),
            P(None, "ch"),
            P("ch"),
        ),
        check_vma=False,
    )
```

profile of v0, /device:TPU:25, one launch (start us, length us, event | category | flops | bytes accessed | tf_op | source)
XLA Modules:
  0.0 444.6 jit_solution(922992032706214905)
XLA Ops:
  7.2 0.0 copy-start
  7.2 0.0 all-gather.5.cloned.1.call-start
  7.2 0.7 all-gather.5.cloned.1.call-update
  7.9 0.0 all-gather.3.cloned.1.call-start
  8.0 1.4 pad_maximum_fusion.5
  9.4 0.0 all-gather.3.cloned.1.call-update
  9.4 0.0 reduce-scatter.2.cloned.1.call-start
  9.5 1.3 dynamic-slice
  11.4 0.9 dynamic-update-slice
  12.3 19.7 %all-reduce.1 = f32[1536]{0:T(1024)S(1)} all-reduce(f32[1536]{0:T(1024)S(1)} %dynamic-update-slice), channel_id=1, replica_groups=mesh['seq'=64,'ch'=8] {'ch'}, use_global_device_ids=true, to_apply=%add.1 | all-reduce | flops 1536 | bytes 12288
  32.0 22.1 %all-gather.5.cloned.1.call-done = bf16[1536,512]{1,0:T(8,128)(2,1)} async-done(((bf16[192,512]{1,0:T(8,128)(2,1)}), bf16[1536,512]{1,0:T(8,128)(2,1)}) %all-gather.5.cloned.1.call-update) | async-done | bytes 1572880 | tf_op jit(solution)/shard_map/all_gather | solution.py:52
  54.1 1.8 convert_reduce_fusion
  55.9 0.1 copy-done.1
  56.0 0.5 fusion.2
  56.5 84.5 %all-gather.3.cloned.1.call-done = bf16[1536,384]{1,0:T(8,128)(2,1)} async-done(((bf16[24,384]{1,0:T(8,128)(2,1)}), bf16[1536,384]{1,0:T(8,128)(2,1)}) %all-gather.3.cloned.1.call-update) | async-done | bytes 1179664 | tf_op jit(solution)/shard_map/all_gather | solution.py:60
  141.0 2.1 fusion.29
  143.2 0.0 copy-start.5
  143.2 0.1 multiply_convert_fusion.5
  143.3 0.1 fusion.46
  143.4 2.2 collective-permute-start.1
  145.5 3.4 collective-permute-start
  149.0 0.0 collective-permute-done.1
  149.0 1.1 collective-permute-done
  150.1 0.8 fusion.33
  151.0 0.4 reshape.57
  151.4 0.4 copy.24
  151.8 0.0 copy-done
  151.8 0.0 copy-done.5
  151.9 2.0 convolution_select_fusion.1
  153.9 1.4 copy.36
  155.3 1.0 reshape.55
  156.3 2.0 multiply_convert_fusion.3
  158.3 0.1 fusion.45
  158.4 6.4 %collective-permute-start.3 = (bf16[192,15]{1,0:T(8,128)(2,1)S(1)}, bf16[192,15]{1,0:T(8,128)(2,1)S(1)}, u32[]{:S(2)}, u32[]{:S(2)}) collective-permute-start(bf16[192,15]{1,0:T(8,128)(2,1)S(1)} %get-tuple-element.18), channel_id=1, source_target_pairs={{8,0},{16,8},{24,16},{32,24},{40,32},{48,40},{56,48},{64,56},{72,6... | collective-permute-start | bytes 17288 | tf_op jit(solution)/shard_map/ppermute | solution.py:17
  164.8 1.9 collective-permute-start.2
  166.7 0.0 collective-permute-done.3
  166.8 1.2 collective-permute-done.2
  167.9 0.1 maximum_bitcast_fusion
  168.1 0.4 reshape.58
  168.5 0.4 copy.30
  169.0 2.0 convolution_select_fusion
  171.0 1.4 copy.37
  172.4 1.0 reshape.56
  173.5 1.2 multiply_convert_fusion.2
  174.6 3.4 convolution_convert_fusion
  178.0 0.0 reduce-scatter.2.cloned.1.call-update
  178.0 0.0 copy-start.2
  178.1 0.2 all-reduce.4.cloned.1.call-start
  178.3 2.1 fusion
  180.4 0.9 copy.34
  181.3 0.4 copy.35
  181.7 2.2 fusion.48
  184.0 0.0 copy-start.4
  184.0 2.4 fusion.28
  186.4 37.6 %reduce-scatter.2.cloned.1.call-done = bf16[192,512]{1,0:T(8,128)(2,1)} async-done(((bf16[1536,512]{1,0:T(8,128)(2,1)}), bf16[192,512]{1,0:T(8,128)(2,1)}) %reduce-scatter.2.cloned.1.call-update) | async-done | bytes 196624 | tf_op jit(solution)/shard_map/reduce_scatter | solution.py:87
  224.0 1.3 fusion.24
  225.3 3.3 pad_maximum_fusion
  228.6 0.0 all-reduce.4.cloned.1.call-update
  228.6 12.6 %psum.14 = f32[2,512]{1,0:T(2,128)S(1)} all-reduce(f32[2,512]{1,0:T(2,128)S(1)} %pad_maximum_fusion.6), channel_id=1, replica_groups=mesh['seq'=64,'ch'=8] {'ch'}, use_global_device_ids=true, to_apply=%region_5.0 | all-reduce | flops 1024 | bytes 8192 | tf_op jit(solution)/shard_map/psum | solution.py:98
  241.2 1.8 fusion.23
  243.0 190.9 %all-reduce.4.cloned.1.call-done = f32[1568,384]{1,0:T(8,128)} async-done(((f32[1568,384]{1,0:T(8,128)}), f32[1568,384]{1,0:T(8,128)}) %all-reduce.4.cloned.1.call-update) | async-done | bytes 2408464 | tf_op jit(solution)/shard_map/psum | solution.py:106
  433.9 1.4 slice.64
  435.3 1.3 slice.65
  436.5 1.5 fusion.44
  (17 shorter events, 0.2 us)
Async XLA Ops:
  7.2 144.7 %copy-start = (f32[31,192]{1,0:T(8,128)S(1)}, f32[31,192]{1,0:T(8,128)}, u32[]{:S(2)}) copy-start(f32[31,192]{1,0:T(8,128)} %param.10) | copy-start | bytes 71428
  7.2 46.9 %all-gather.5.cloned.1.call-start = ((), (), s32[]{:S(2)}) async-start(), calls=%async_computation.2 | async-start | bytes 1769472 | tf_op jit(solution)/shard_map/all_gather | solution.py:52
  7.9 133.1 %all-gather.3.cloned.1.call-start = ((), (), s32[]{:S(2)}) async-start(), calls=%async_computation.1 | async-start | bytes 1198080 | tf_op jit(solution)/shard_map/all_gather | solution.py:60
  9.4 214.6 %reduce-scatter.2.cloned.1.call-start = ((), (), s32[]{:S(2)}) async-start(), calls=%async_computation.3 | async-start | bytes 1769472 | tf_op jit(solution)/shard_map/reduce_scatter | solution.py:87
  54.1 1.9 copy-start.1
  143.2 8.7 %copy-start.5 = (pred[8,68]{0,1:T(8,128)(4,1)S(1)}, pred[8,68]{0,1:T(8,128)(4,1)}, u32[]{:S(2)}) copy-start(pred[8,68]{0,1:T(8,128)(4,1)} %constant.49) | copy-start | bytes 1636
  143.4 5.6 %collective-permute-start.1 = (bf16[192,15]{1,0:T(8,128)(2,1)S(1)}, bf16[192,15]{1,0:T(8,128)(2,1)S(1)}, u32[]{:S(2)}, u32[]{:S(2)}) collective-permute-start(bf16[192,15]{1,0:T(8,128)(2,1)S(1)} %get-tuple-element.20), channel_id=1, source_target_pairs={{8,0},{16,8},{24,16},{32,24},{40,32},{48,40},{56,48},{64,56},{72,6... | collective-permute-start | bytes 17288 | tf_op jit(solution)/shard_map/ppermute | solution.py:17
  145.5 4.6 %collective-permute-start = (bf16[192,15]{1,0:T(8,128)(2,1)S(1)}, bf16[192,15]{1,0:T(8,128)(2,1)S(1)}, u32[]{:S(2)}, u32[]{:S(2)}) collective-permute-start(bf16[192,15]{1,0:T(8,128)(2,1)S(1)} %get-tuple-element.19), channel_id=1, source_target_pairs={{0,8},{8,16},{16,24},{24,32},{32,40},{40,48},{48,56},{56,64},{64,7... | collective-permute-start | bytes 17288 | tf_op jit(solution)/shard_map/ppermute | solution.py:15
  158.4 8.4 %collective-permute-start.3 = (bf16[192,15]{1,0:T(8,128)(2,1)S(1)}, bf16[192,15]{1,0:T(8,128)(2,1)S(1)}, u32[]{:S(2)}, u32[]{:S(2)}) collective-permute-start(bf16[192,15]{1,0:T(8,128)(2,1)S(1)} %get-tuple-element.18), channel_id=1, source_target_pairs={{8,0},{16,8},{24,16},{32,24},{40,32},{48,40},{56,48},{64,56},{72,6... | collective-permute-start | bytes 17288 | tf_op jit(solution)/shard_map/ppermute | solution.py:17
  164.8 3.1 collective-permute-start.2
  178.0 2.4 copy-start.2
  178.1 255.9 %all-reduce.4.cloned.1.call-start = ((), (), s32[]{:S(2)}) async-start(), calls=%async_computation.4 | async-start | bytes 4816896 | tf_op jit(solution)/shard_map/psum | solution.py:106
  184.0 40.0 %copy-start.4 = (f32[192]{0:T(256)S(1)}, f32[192]{0:T(256)}, u32[]{:S(2)}) copy-start(f32[192]{0:T(256)} %param.7) | copy-start | bytes 2308
  228.6 12.6 %copy-start.3 = (bf16[192,512]{1,0:T(8,128)(2,1)S(1)}, bf16[192,512]{1,0:T(8,128)(2,1)}, u32[]{:S(2)}) copy-start(bf16[192,512]{1,0:T(8,128)(2,1)} %reduce-scatter.2.cloned.1.call-done) | copy-start | bytes 589828
Sparse Core Ops, SparseCore 0:
  10.1 43.9 all-gather.4
  57.9 83.0 all-gather.2
  178.2 45.7 reduce-scatter.1
  228.7 205.1 all-reduce.3
where the time goes:
time: 445 us
  waiting for transfers between devices  338 us (76%)
  blocking collectives  32.2 us (7%)
  other arithmetic  16.4 us (4%)
  between operations  14.7 us (3%)
  local copies, waits for them, and re-layouts  14.5 us (3%)
  starting transfers between devices  14.3 us (3%)
  matrix products  14.2 us (3%)
    psum x1, waiting for transfers between devices, shards(): summed = lax.psum(jnp.concatenate([weight_partial, extra], 0), 'seq')  191 us
    all_gather x1, waiting for transfers between devices, shards(): gathered = lax.all_gather(stacked, 'seq', axis=0, tiled=True)  84.5 us
    reduce_scatter x1, waiting for transfers between devices, shards(): lax.psum_scatter(normed_term.astype(jnp.bfloat16), 'ch', scatter_dimensio...  37.6 us
    all_gather x1, waiting for transfers between devices, shards(): complete_signal = lax.all_gather(signal, 'ch', axis=0, tiled=True)  22.1 us
    unnamed x1, blocking collectives  19.7 us
    psum x1, blocking collectives, shards(): moments = lax.psum(moments, 'ch') * (1.0 / complete_signal.shape[0])  12.6 us
  transfers between devices with their start and end apart: 8, of which 6 were waited for; matrix products, arithmetic and copies ran while one was open for 4% of the time, Pallas kernels for 0%

commit v1 on v0

--- a/solution.py
+++ b/solution.py
@@ -49,7 +49,9 @@
     seq_position = lax.axis_index("seq")
     channel_position = lax.axis_index("ch")
     reach = depth_taps.shape[0] // 2
-    complete_signal = lax.all_gather(signal, "ch", axis=0, tiled=True)
+    complete_signal = jnp.concatenate(
+        lax.all_to_all(jnp.stack([signal] * lax.axis_size("ch")), "ch", 0, 0), axis=0
+    )
     complete_gain = lax.all_gather(input_norm_gain, "ch", axis=0, tiled=True)
     centered_unit, inverse_deviation = standardize_rows(complete_signal)
     normalized_signal = (centered_unit * complete_gain[:, None]).astype(jnp.bfloat16)

time: 445 us -> 410 us (0.921)
  waiting for transfers between devices: 338 us -> 271 us
  blocking collectives: 32.2 us -> 54.6 us
  starting transfers between devices: 14.3 us -> 24.2 us
    all_gather x1, waiting for transfers between devices: 84.5 us -> 38.8 us  [shards(): gathered = lax.all_gather(stacked, 'seq', axis=0, tiled=True)]
    unnamed x1, blocking collectives: 19.7 us -> 42.5 us
    all_gather x1 -> x0, waiting for transfers between devices: 22.1 us -> none  [shards(): complete_signal = lax.all_gather(signal, 'ch', axis=0, tiled=True)]
    all_to_all x0 -> x1, starting transfers between devices: none -> 10 us  [shards(): lax.all_to_all(jnp.stack([signal] * lax.axis_size('ch')), 'ch', 0, 0)]
  transfers between devices with their start and end apart: 8 -> 8, of which waited for: 6 -> 5; matrix products, arithmetic and copies ran while one was open for 4% -> 3% of each run, Pallas kernels for 0% -> 0%
where the time goes in v1:
time: 410 us
  waiting for transfers between devices  271 us (66%)
  blocking collectives  54.6 us (13%)
  starting transfers between devices  24.2 us (6%)
  local copies, waits for them, and re-layouts  16.1 us (4%)
  between operations  14.7 us (4%)
  other arithmetic  14.2 us (3%)
  matrix products  14.2 us (3%)
    psum x1, waiting for transfers between devices, shards(): summed = lax.psum(jnp.concatenate([weight_partial, extra], 0), 'seq')  190 us
    unnamed x1, blocking collectives  42.5 us
    reduce_scatter x1, waiting for transfers between devices, shards(): lax.psum_scatter(normed_term.astype(jnp.bfloat16), 'ch', scatter_dimensio...  39.7 us
    all_gather x1, waiting for transfers between devices, shards(): gathered = lax.all_gather(stacked, 'seq', axis=0, tiled=True)  38.8 us
    psum x1, blocking collectives, shards(): moments = lax.psum(moments, 'ch') * (1.0 / complete_signal.shape[0])  12.1 us
    all_to_all x1, starting transfers between devices, shards(): lax.all_to_all(jnp.stack([signal] * lax.axis_size('ch')), 'ch', 0, 0)  10 us
    ppermute x2, starting transfers between devices, extended(): lax.ppermute(head, axis, [((i + 1) % count, i) for i in range(ends)])  8.58 us
  transfers between devices with their start and end apart: 8, of which 5 were waited for; matrix products, arithmetic and copies ran while one was open for 3% of the time, Pallas kernels for 0%

profile of v1, /device:TPU:25, one launch (start us, length us, event | category | flops | bytes accessed | tf_op | source)
XLA Modules:
  0.0 409.5 jit_solution(5130993227094594396)
XLA Ops:
  7.2 0.0 copy-start
  7.2 0.0 copy-start.3
  7.2 2.2 stack.2
  9.5 10.0 %all-to-all-start = ((bf16[8,192,512]{2,1,0:T(8,128)(2,1)}), bf16[8,192,512]{2,1,0:T(8,128)(2,1)S(1)}, u32[]{:S(2)}, u32[]{:S(2)}) async-start(bf16[8,192,512]{2,1,0:T(8,128)(2,1)} %stack.2), calls=%async_computation | async-start | bytes 3145728 | tf_op jit(solution)/shard_map/all_to_all | solution.py:53
  19.5 0.0 all-gather.2.cloned.1.call-start
  19.6 0.7 pad_maximum_fusion.5
  20.2 0.0 all-gather.2.cloned.1.call-update
  20.3 0.0 reduce-scatter.2.cloned.1.call-start
  20.3 1.3 dynamic-slice
  22.3 0.0 copy-done.5
  22.3 0.3 dynamic-update-slice
  22.6 42.5 %all-reduce.1 = f32[1536]{0:T(1024)S(1)} all-reduce(f32[1536]{0:T(1024)S(1)} %dynamic-update-slice), channel_id=1, replica_groups=mesh['seq'=64,'ch'=8] {'ch'}, use_global_device_ids=true, to_apply=%add.1 | all-reduce | flops 1536 | bytes 12288
  65.1 0.0 all-to-all-done
  65.1 0.3 convert_reduce_fusion
  65.4 0.5 multiply_reduce_fusion
  65.9 2.1 fusion
  68.0 38.8 %all-gather.2.cloned.1.call-done = bf16[1536,384]{1,0:T(8,128)(2,1)} async-done(((bf16[24,384]{1,0:T(8,128)(2,1)}), bf16[1536,384]{1,0:T(8,128)(2,1)}) %all-gather.2.cloned.1.call-update) | async-done | bytes 1179664 | tf_op jit(solution)/shard_map/all_gather | solution.py:62
  106.8 2.1 fusion.46
  108.9 0.0 copy-start.6
  108.9 0.1 multiply_convert_fusion.5
  109.0 0.1 fusion.43
  109.1 2.1 collective-permute-start.1
  111.2 3.4 collective-permute-start
  114.7 0.0 collective-permute-done.1
  114.7 1.1 collective-permute-done
  115.8 0.9 fusion.30
  116.7 0.4 reshape.68
  117.1 0.4 copy.24
  117.5 0.0 copy-done
  117.6 0.0 copy-done.6
  117.6 2.0 convolution_select_fusion.1
  119.6 1.4 copy.36
  121.0 1.0 reshape.66
  122.1 2.0 multiply_convert_fusion.3
  124.0 0.1 fusion.42
  124.1 6.4 %collective-permute-start.3 = (bf16[192,15]{1,0:T(8,128)(2,1)S(1)}, bf16[192,15]{1,0:T(8,128)(2,1)S(1)}, u32[]{:S(2)}, u32[]{:S(2)}) collective-permute-start(bf16[192,15]{1,0:T(8,128)(2,1)S(1)} %get-tuple-element.20), channel_id=1, source_target_pairs={{8,0},{16,8},{24,16},{32,24},{40,32},{48,40},{56,48},{64,56},{72,6... | collective-permute-start | bytes 17288 | tf_op jit(solution)/shard_map/ppermute | solution.py:17
  130.5 1.9 collective-permute-start.2
  132.5 0.0 collective-permute-done.3
  132.5 1.2 collective-permute-done.2
  133.7 0.1 maximum_bitcast_fusion
  133.9 0.4 reshape.69
  134.3 0.4 copy.30
  134.7 2.0 convolution_select_fusion
  136.7 1.4 copy.37
  138.2 1.0 reshape.67
  139.2 1.2 multiply_convert_fusion.2
  140.4 3.4 convolution_convert_fusion
  143.8 0.0 reduce-scatter.2.cloned.1.call-update
  143.8 0.2 all-reduce.4.cloned.1.call-start
  144.1 0.9 copy.34
  145.0 0.4 copy.35
  145.4 2.2 fusion.45
  147.7 2.4 fusion.26
  150.1 39.7 %reduce-scatter.2.cloned.1.call-done = bf16[192,512]{1,0:T(8,128)(2,1)} async-done(((bf16[1536,512]{1,0:T(8,128)(2,1)}), bf16[192,512]{1,0:T(8,128)(2,1)}) %reduce-scatter.2.cloned.1.call-update) | async-done | bytes 196624 | tf_op jit(solution)/shard_map/reduce_scatter | solution.py:89
  189.8 1.3 fusion.22
  191.1 3.3 pad_maximum_fusion
  194.4 0.0 all-reduce.4.cloned.1.call-update
  194.5 12.1 %psum.14 = f32[2,512]{1,0:T(2,128)S(1)} all-reduce(f32[2,512]{1,0:T(2,128)S(1)} %pad_maximum_fusion.6), channel_id=1, replica_groups=mesh['seq'=64,'ch'=8] {'ch'}, use_global_device_ids=true, to_apply=%region_5.0 | all-reduce | flops 1024 | bytes 8192 | tf_op jit(solution)/shard_map/psum | solution.py:100
  206.6 0.0 copy-done.2
  206.6 1.8 fusion.21
  208.4 190.5 %all-reduce.4.cloned.1.call-done = f32[1568,384]{1,0:T(8,128)} async-done(((f32[1568,384]{1,0:T(8,128)}), f32[1568,384]{1,0:T(8,128)}) %all-reduce.4.cloned.1.call-update) | async-done | bytes 2408464 | tf_op jit(solution)/shard_map/psum | solution.py:108
  398.9 1.4 slice.64
  400.2 1.3 slice.65
  401.5 1.5 fusion.41
  (19 shorter events, 0.2 us)
Async XLA Ops:
  7.2 110.4 %copy-start = (f32[31,192]{1,0:T(8,128)S(1)}, f32[31,192]{1,0:T(8,128)}, u32[]{:S(2)}) copy-start(f32[31,192]{1,0:T(8,128)} %param.10) | copy-start | bytes 71428
  7.2 12.4 %copy-start.3 = (bf16[24,192]{1,0:T(8,128)(2,1)S(1)}, bf16[24,192]{1,0:T(8,128)(2,1)}, u32[]{:S(2)}) copy-start(bf16[24,192]{1,0:T(8,128)(2,1)} %param.9) | copy-start | bytes 27652
  7.2 12.4 %copy-start.4 = (bf16[24,192]{1,0:T(8,128)(2,1)S(1)}, bf16[24,192]{1,0:T(8,128)(2,1)}, u32[]{:S(2)}) copy-start(bf16[24,192]{1,0:T(8,128)(2,1)} %param.8) | copy-start | bytes 27652
  7.2 15.1 %copy-start.5 = (f32[192]{0:T(256)S(1)}, f32[192]{0:T(256)}, u32[]{:S(2)}) copy-start(f32[192]{0:T(256)} %param.7) | copy-start | bytes 2308
  9.5 55.6 %all-to-all-start = ((bf16[8,192,512]{2,1,0:T(8,128)(2,1)}), bf16[8,192,512]{2,1,0:T(8,128)(2,1)S(1)}, u32[]{:S(2)}, u32[]{:S(2)}) async-start(bf16[8,192,512]{2,1,0:T(8,128)(2,1)} %stack.2), calls=%async_computation | async-start | bytes 3145728 | tf_op jit(solution)/shard_map/all_to_all | solution.py:53
  19.5 87.3 %all-gather.2.cloned.1.call-start = ((), (), s32[]{:S(2)}) async-start(), calls=%async_computation.2 | async-start | bytes 1198080 | tf_op jit(solution)/shard_map/all_gather | solution.py:62
  20.3 169.6 %reduce-scatter.2.cloned.1.call-start = ((), (), s32[]{:S(2)}) async-start(), calls=%async_computation.3 | async-start | bytes 1769472 | tf_op jit(solution)/shard_map/reduce_scatter | solution.py:89
  108.9 8.7 %copy-start.6 = (pred[8,68]{0,1:T(8,128)(4,1)S(1)}, pred[8,68]{0,1:T(8,128)(4,1)}, u32[]{:S(2)}) copy-start(pred[8,68]{0,1:T(8,128)(4,1)} %constant.49) | copy-start | bytes 1636
  109.1 5.6 %collective-permute-start.1 = (bf16[192,15]{1,0:T(8,128)(2,1)S(1)}, bf16[192,15]{1,0:T(8,128)(2,1)S(1)}, u32[]{:S(2)}, u32[]{:S(2)}) collective-permute-start(bf16[192,15]{1,0:T(8,128)(2,1)S(1)} %get-tuple-element.22), channel_id=1, source_target_pairs={{8,0},{16,8},{24,16},{32,24},{40,32},{48,40},{56,48},{64,56},{72,6... | collective-permute-start | bytes 17288 | tf_op jit(solution)/shard_map/ppermute | solution.py:17
  111.2 4.6 %collective-permute-start = (bf16[192,15]{1,0:T(8,128)(2,1)S(1)}, bf16[192,15]{1,0:T(8,128)(2,1)S(1)}, u32[]{:S(2)}, u32[]{:S(2)}) collective-permute-start(bf16[192,15]{1,0:T(8,128)(2,1)S(1)} %get-tuple-element.21), channel_id=1, source_target_pairs={{0,8},{8,16},{16,24},{24,32},{32,40},{40,48},{48,56},{56,64},{64,7... | collective-permute-start | bytes 17288 | tf_op jit(solution)/shard_map/ppermute | solution.py:15
  124.1 8.4 %collective-permute-start.3 = (bf16[192,15]{1,0:T(8,128)(2,1)S(1)}, bf16[192,15]{1,0:T(8,128)(2,1)S(1)}, u32[]{:S(2)}, u32[]{:S(2)}) collective-permute-start(bf16[192,15]{1,0:T(8,128)(2,1)S(1)} %get-tuple-element.20), channel_id=1, source_target_pairs={{8,0},{16,8},{24,16},{32,24},{40,32},{48,40},{56,48},{64,56},{72,6... | collective-permute-start | bytes 17288 | tf_op jit(solution)/shard_map/ppermute | solution.py:17
  130.5 3.1 collective-permute-start.2
  140.4 3.7 copy-start.1
  143.8 255.0 %all-reduce.4.cloned.1.call-start = ((), (), s32[]{:S(2)}) async-start(), calls=%async_computation.4 | async-start | bytes 4816896 | tf_op jit(solution)/shard_map/psum | solution.py:108
  194.4 12.1 %copy-start.2 = (bf16[192,512]{1,0:T(8,128)(2,1)S(1)}, bf16[192,512]{1,0:T(8,128)(2,1)}, u32[]{:S(2)}) copy-start(bf16[192,512]{1,0:T(8,128)(2,1)} %reduce-scatter.2.cloned.1.call-done) | copy-start | bytes 589828
Sparse Core Ops, SparseCore 0:
  24.2 82.5 all-gather.1
  144.0 45.8 reduce-scatter.1
  194.6 204.2 all-reduce.3
